TPU v7x, 256 devices: a whole 4x4x8 slice. The times are simulated.
256 devices in a mesh: tok: 16 (over z, core), tp: 16 (over x, y).
Axes of the slice: x: 4, y: 4, z: 8, core: 2. Of those that a mesh axis runs over, the one named last changes fastest.
Arguments:
- hidden_states: bfloat16 [32768, 1024], P(('tok', 'tp')), may hold values from -40 to 40
- first_gain: float32 [1024], replicated, may hold values from 0.1 to 1.9
- second_gain: float32 [1024], replicated, may hold values from 0.1 to 1.9
- w_query: bfloat16 [1024, 1024], P(None, 'tp'), may hold values from -1 to 1
- w_keyval: bfloat16 [1024, 1024], replicated, may hold values from -0.375 to 0.375
- w_out: bfloat16 [1024, 1024], P('tp'), may hold values from -0.75 to 0.75
- kv_cache: bfloat16 [384, 128, 1024], P('tok'), may hold values from -310 to 310
- page_table: int32 [32, 16], P('tok'), may hold values from 0 to 383, as said below
- cached_len: int32 [32], P('tok'), may hold values from 128 to 2048, as said below
- expert_ids: int32 [32768, 8], P(('tok', 'tp')), may hold values from 0 to 31, all different within a row; in each aligned block of 128 rows (0 to 127, 128 to 255, ...) at most 64 rows name the same one
- gate_weights: float32 [32768, 8], P(('tok', 'tp')), may hold values from 0.1 to 1
- w_gate_up: bfloat16 [32, 1024, 1024], P('tp', 'tok'), may hold values from -0.1875 to 0.1875
- w_down: bfloat16 [32, 512, 1024], P('tp', 'tok'), may hold values from -1 to 1
Outputs:
- layer_out: bfloat16 [32768, 1024], P(('tok', 'tp'))
Inputs may be any that keep to these rules, and one draw needn't show every extreme that they name: `page_table`: request r's entries are pages of its own tok index, rows 24 * (r // 2) to 24 * (r // 2 + 1) - 1; its first 8 entries are the same for all requests of that tok index, and all other entries name pages that no other entry names. `cached_len`: some request has exactly 2048 cached tokens. `expert_ids`: in the rows of one device (aligned blocks of 128 rows) no expert is named by more than 64 rows, and a row names 8 different experts.
All inputs are finite; a program needn't handle non-finite values.
Results may differ from a plain program's by a relative error of at most 0.017.
The roundings to bfloat16 on the way count: a program that leaves them out, or rounds other values in their place, can miss the bound.
Values may be sent and summed in bfloat16 or wider, within the bound.
No kernel may reach another device: no remote copies, remote signals or barrier semaphores. Data moves between devices by JAX's collectives and lax.ppermute only.
A program may use at most 128 MiB of HBM per device.

v0:
```python
import jax
import jax.numpy as jnp
from jax import lax
from jax.sharding import Mesh
from jax.sharding import PartitionSpec as P

D = 1024
HEADS = 16
KV_HEADS = 8
HEAD_DIM = 64
EXPERTS = 32
FF_EXPERT = 512
TOP = 8
NEW = 1024
MAX_CACHED = 2048
REQ_DEV = 2
ATTN_SCALE = 0.015625
EPSILON = 1e-06
THETA = 10000.0
TOK = ("tz", "tc")
TP = ("ra", "rb")


def rms_norm(values, gain):
    wide = values.astype(jnp.float32)
    factor = lax.rsqrt(jnp.mean(wide * wide, axis=-1, keepdims=True) + EPSILON)
    return (wide * factor * gain).astype(jnp.bfloat16)


def rotate(values, positions):
    row_count = values.shape[0]
    shaped = values.reshape(row_count, -1, HEAD_DIM)
    half_dim = HEAD_DIM // 2
    exponent = jnp.arange(half_dim).astype(jnp.float32) * (2.0 / HEAD_DIM)
    frequency = jnp.power(THETA, -exponent)
    angles = positions.astype(jnp.float32)[:, None] * frequency[None, :]
    cosine = jnp.cos(angles)[:, None, :]
    sine_part = jnp.sin(angles)[:, None, :]
    leading = shaped[..., :half_dim]
    trailing = shaped[..., half_dim:]
    turned = jnp.concatenate(
        [leading * cosine - trailing * sine_part, trailing * cosine + leading * sine_part], axis=-1
    )
    return turned.reshape(row_count, -1)


def shards(
    hidden_states,
    first_gain,
    second_gain,
    w_query,
    w_keyval,
    w_out,
    kv_cache,
    page_table,
    cached_len,
    expert_ids,
    gate_weights,
    w_gate_up,
    w_down,
):
    tok_rows = hidden_states.shape[0]
    tp_size = lax.axis_size(TP)
    core = lax.axis_index("tc")
    local_req = lax.axis_index("ra")
    block = lax.axis_index("rb")
    kv_cols = KV_HEADS * HEAD_DIM
    group_size = HEADS // KV_HEADS
    half_rows = D // 2
    wq_half = lax.dynamic_slice_in_dim(w_query, core * half_rows, half_rows, 0)
    wq_full = lax.all_gather(
        lax.all_gather(wq_half, TP, axis=1, tiled=True), "tc", axis=0, tiled=True
    )
    wo_half = lax.dynamic_slice_in_dim(w_out, core * half_rows, half_rows, 1)
    wo_full = lax.all_gather(
        lax.all_gather(wo_half, TP, axis=0, tiled=True), "tc", axis=1, tiled=True
    )
    gate_up_full = lax.all_gather(w_gate_up, TOK, axis=1, tiled=True)
    down_full = lax.all_gather(w_down, TOK, axis=1, tiled=True)
    normed = rms_norm(hidden_states, first_gain)
    length = cached_len[local_req]
    positions = length + block * tok_rows + jnp.arange(tok_rows, dtype=jnp.int32)
    keyval = jnp.dot(normed, w_keyval, preferred_element_type=jnp.float32)
    new_kv = jnp.concatenate(
        [rotate(keyval[:, :kv_cols], positions), keyval[:, kv_cols:]], axis=1
    ).astype(jnp.bfloat16)
    request_kv = lax.all_gather(new_kv, "rb", axis=0, tiled=True)
    queries = rotate(
        jnp.dot(normed, wq_full, preferred_element_type=jnp.float32), positions
    ).astype(jnp.bfloat16)
    local_pages = page_table[local_req] - lax.axis_index(TOK) * kv_cache.shape[0]
    cached = jnp.take(kv_cache, local_pages, axis=0).reshape(MAX_CACHED, 2 * kv_cols)
    keys_total = jnp.concatenate([cached[:, :kv_cols], request_kv[:, :kv_cols]], axis=0).reshape(
        MAX_CACHED + NEW, KV_HEADS, HEAD_DIM
    )
    values_total = jnp.concatenate([cached[:, kv_cols:], request_kv[:, kv_cols:]], axis=0).reshape(
        MAX_CACHED + NEW, KV_HEADS, HEAD_DIM
    )
    grouped_q = queries.reshape(tok_rows, KV_HEADS, group_size, HEAD_DIM)
    scores = (
        jnp.einsum("qgpd,kgd->gpqk", grouped_q, keys_total, preferred_element_type=jnp.float32)
        * ATTN_SCALE
    )
    key_index = jnp.arange(MAX_CACHED + NEW, dtype=jnp.int32)
    query_pos = block * tok_rows + jnp.arange(tok_rows, dtype=jnp.int32)
    allowed = jnp.where(
        key_index[None, :] < MAX_CACHED,
        key_index[None, :] < length,
        key_index[None, :] - MAX_CACHED <= query_pos[:, None],
    )
    scores = jnp.where(allowed, scores, -1e30)
    top_score = jnp.max(scores, axis=-1, keepdims=True)
    weights = jnp.exp(scores - top_score)
    probs = (weights / jnp.sum(weights, axis=-1, keepdims=True)).astype(jnp.bfloat16)
    attended = (
        jnp.einsum("gpqk,kgd->qgpd", probs, values_total, preferred_element_type=jnp.float32)
        .astype(jnp.bfloat16)
        .reshape(tok_rows, HEADS * HEAD_DIM)
    )
    projected_out = jnp.dot(attended, wo_full, preferred_element_type=jnp.float32)
    middle = (hidden_states.astype(jnp.float32) + projected_out).astype(jnp.bfloat16)
    normed_two = rms_norm(middle, second_gain)
    experts_local = EXPERTS // tp_size
    capacity = 2 * tok_rows * TOP // EXPERTS
    expert_range = jnp.arange(EXPERTS, dtype=jnp.int32)
    onehot = (expert_ids[:, :, None] == expert_range[None, None, :]).astype(jnp.int32)
    per_token = jnp.sum(onehot, axis=1)
    earlier = jnp.cumsum(per_token, axis=0) - per_token
    slot_ids = jnp.sum(onehot * earlier[:, None, :], axis=2)
    target = expert_ids * capacity + slot_ids
    outgoing_rows = jnp.broadcast_to(normed_two[:, None, :], (tok_rows, TOP, D))
    send_buffer = jnp.zeros((EXPERTS * capacity, D), jnp.bfloat16).at[target].set(outgoing_rows)
    received = lax.all_to_all(
        send_buffer.reshape(tp_size, experts_local, capacity, D),
        TP,
        split_axis=0,
        concat_axis=2,
        tiled=True,
    )
    received = received.reshape(experts_local, tp_size * capacity, D)
    both = jnp.einsum("esd,edf->esf", received, gate_up_full, preferred_element_type=jnp.float32)
    activated = (jax.nn.silu(both[..., :FF_EXPERT]) * both[..., FF_EXPERT:]).astype(jnp.bfloat16)
    produced = jnp.einsum(
        "esf,efd->esd", activated, down_full, preferred_element_type=jnp.float32
    ).astype(jnp.bfloat16)
    returned = lax.all_to_all(
        produced.reshape(experts_local, tp_size, capacity, D),
        TP,
        split_axis=1,
        concat_axis=0,
        tiled=True,
    )
    returned = returned.reshape(EXPERTS * capacity, D)
    picked = returned[target]
    mixture = jnp.einsum("tk,tkd->td", gate_weights, picked.astype(jnp.float32))
    return (middle.astype(jnp.float32) + mixture).astype(jnp.bfloat16)


def solution(mesh):
    tok_size, tp_size = mesh.devices.shape
    group = tp_size // REQ_DEV
    split = Mesh(mesh.devices.reshape(tok_size // 2, 2, REQ_DEV, group), TOK + TP)
    in_specs = (
        P(TOK + TP, None),
        P(),
        P(),
        P(None, TP),
        P(),
        P(TP, None),
        P(TOK, None, None),
        P(TOK, None),
        P(TOK),
        P(TOK + TP, None),
        P(TOK + TP, None),
        P(TP, TOK, None),
        P(TP, TOK, None),
    )
    out_specs = P(TOK + TP, None)
    return jax.shard_map(
        shards, mesh=split, in_specs=in_specs, out_specs=out_specs, check_vma=False
    )
```

profile of v0, /device:TPU:28, one launch (start us, length us, event | category | flops | bytes accessed | tf_op | source)
XLA Modules:
  0.0 387.6 jit_solution(11292400467645476767)
XLA Ops:
  14.9 43.1 %all-gather.10.cloned.1.call-done = bf16[512,1024]{0,1:T(8,128)(2,1)} async-done(((bf16[512,64]{0,1:T(8,128)(2,1)}), bf16[512,1024]{0,1:T(8,128)(2,1)}) %all-gather.10.cloned.1.call-update) | async-done | bytes 1048592 | tf_op jit(solution)/shard_map/all_gather | solution.py:72
  58.1 49.3 %all-gather.14.cloned.1.call-done = bf16[1024,512]{1,0:T(8,128)(2,1)} async-done(((bf16[64,512]{1,0:T(8,128)(2,1)}), bf16[1024,512]{1,0:T(8,128)(2,1)}) %all-gather.14.cloned.1.call-update) | async-done | bytes 1048592 | tf_op jit(solution)/shard_map/all_gather | solution.py:76
  108.7 5.5 %gather_fusion = bf16[16,128,1024]{2,1,0:T(8,128)(2,1)} fusion(bf16[24,128,1024]{2,1,0:T(8,128)(2,1)} %param.19, s32[1024]{0:T(1024)S(1)} %pad_clamp_fusion), kind=kCustom, calls=%fused_computation | custom fusion | bytes 8388672 | tf_op jit(solution)/shard_map/jit(_take)/gather | solution.py:92
  114.3 6.6 %copy.43 = bf16[2048,1024]{0,1:T(8,128)(2,1)} copy(bf16[2048,1024]{1,0:T(8,128)(2,1)} %bitcast.74) | data formatting | bytes 8388608 | tf_op jit(solution)/shard_map/jit(_take)/gather | solution.py:92
  120.9 2.7 broadcast_select_fusion
  125.7 3.5 compare_select_fusion
  129.4 22.4 %all-gather.8.cloned.1.call-done = bf16[1024,1024]{1,0:T(8,128)(2,1)} async-done(((bf16[128,1024]{1,0:T(8,128)(2,1)}), bf16[1024,1024]{1,0:T(8,128)(2,1)}) %all-gather.8.cloned.1.call-update) | async-done | bytes 2097168 | tf_op jit(solution)/shard_map/all_gather | solution.py:87
  151.9 3.0 fusion.34
  158.6 4.3 %pad_maximum_fusion = (bf16[3072,512]{0,1:T(8,128)(2,1)}, bf16[3072,512]{0,1:T(8,128)(2,1)}) fusion(bf16[1024,512]{0,1:T(8,128)(2,1)S(1)} %copy.46, bf16[2048,512]{0,1:T(8,128)(2,1)} %get-tuple-element.6, bf16[1024,512]{0,1:T(8,128)(2,1)} %copy.47, bf16[2048,512]{0,1:T(8,128)(2,1)S(1)} %get-tuple-element.5), kind=kLoop, calls=%fused_computation.15 | loop fusion | flops 12582912 | bytes 12582912 | tf_op jit(solution)/shard_map/concatenate | solution.py:96
  162.9 8.4 %all-gather.12.cloned.1.call-done = bf16[1024,1024]{0,1:T(8,128)(2,1)} async-done(((bf16[512,1024]{0,1:T(8,128)(2,1)}), bf16[1024,1024]{0,1:T(8,128)(2,1)}) %all-gather.12.cloned.1.call-update) | async-done | bytes 2097168 | tf_op jit(solution)/shard_map/all_gather | solution.py:71
  171.3 2.4 fusion.24
  173.8 14.0 %fusion.35 = (f32[8,2,128]{2,1,0:T(2,128)S(1)}, f32[8,2,128,3072]{2,3,1,0:T(8,128)}) fusion(pred[128,3072]{0,1:T(8,128)(4,1)S(1)} %copy-done.3, bf16[3072,8,64,1]{0,2,3,1:T(8,128)(2,1)} %bitcast.78, bf16[128,8,2,64]{0,3,2,1:T(8,128)(2,1)S(1)} %bitcast.82), kind=kOutput, calls=%fused_computation.80 | convolution fusion | flops 830475264 | bytes 28975104 | tf_op jit(solution)/shard_map/sub | solution.py:113
  187.8 11.7 %fusion.18 = bf16[8,64,2,128]{3,1,2,0:T(8,128)(2,1)S(1)} fusion(bf16[3072,8,64,1]{0,2,3,1:T(8,128)(2,1)} %bitcast.77, f32[8,2,128,3072]{2,3,1,0:T(8,128)} %get-tuple-element.16, f32[8,2,128]{2,1,0:T(2,128)S(1)} %get-tuple-element.15), kind=kOutput, calls=%fused_computation.29 | convolution fusion | flops 818020352 | bytes 28581888 | tf_op jit(solution)/shard_map/gpqk,kgd->qgpd/dot_general | solution.py:116
  201.8 8.1 %scatter_custom_fusion = bf16[2048,1024]{1,0:T(8,128)(2,1)} fusion(s32[1024]{0:T(1024)S(1)} %reshape.206, bf16[]{:T(256)} %constant.75.clone.1, bf16[128,1024]{1,0:T(8,128)(2,1)S(1)} %multiply_convert_fusion), kind=kCustom, calls=%fused_computation.21 | custom fusion | bytes 4456450 | tf_op jit(solution)/shard_map/scatter | solution.py:132
  210.0 7.2 %all-to-all-start = ((bf16[16,2,64,1024]{3,2,1,0:T(8,128)(2,1)}), bf16[16,2,64,1024]{3,2,1,0:T(8,128)(2,1)}, u32[]{:S(2)}, u32[]{:S(2)}) async-start(bf16[16,2,64,1024]{3,2,1,0:T(8,128)(2,1)} %bitcast.73), calls=%async_computation | async-start | bytes 8388608 | tf_op jit(solution)/shard_map/all_to_all | solution.py:133
  217.9 61.8 %all-to-all-done = bf16[16,2,64,1024]{3,2,1,0:T(8,128)(2,1)} async-done(((bf16[16,2,64,1024]{3,2,1,0:T(8,128)(2,1)}), bf16[16,2,64,1024]{3,2,1,0:T(8,128)(2,1)}, u32[]{:S(2)}, u32[]{:S(2)}) %all-to-all-start) | async-done | bytes 4194336 | tf_op jit(solution)/shard_map/all_to_all | solution.py:133
  279.7 4.9 %copy.54 = bf16[1,2,16,64,1024]{4,3,2,1,0:T(8,128)(2,1)} copy(bf16[1,2,16,64,1024]{4,3,1,2,0:T(8,128)(2,1)} %bitcast.22) | data formatting | bytes 8388608 | tf_op jit(solution)/shard_map/all_to_all | solution.py:133
  284.6 11.2 %fusion.36 = f32[2,1024,1024]{2,1,0:T(8,128)} fusion(bf16[2,1024,1024]{2,1,0:T(8,128)(2,1)} %bitcast.75, bf16[2,1024,1024]{2,1,0:T(8,128)(2,1)} %all-gather.18.cloned.1.call-done), kind=kOutput, calls=%fused_computation.81 | convolution fusion | flops 4294967296 | bytes 16777216 | tf_op jit(solution)/shard_map/esd,edf->esf/dot_general | solution.py:141
  295.8 6.4 %convolution_convert_fusion = bf16[2,1024,1024]{2,1,0:T(8,128)(2,1)S(1)} fusion(bf16[2,512,1024]{2,1,0:T(8,128)(2,1)} %all-gather.20.cloned.1.call-done, f32[2,1024,1024]{2,1,0:T(8,128)} %fusion.36), kind=kOutput, calls=%fused_computation.18 | convolution fusion | flops 2155872256 | bytes 14680064 | tf_op jit(solution)/shard_map/esf,efd->esd/dot_general | solution.py:143
  302.2 2.5 copy.55
  304.7 7.9 %all-to-all-start.1 = ((bf16[2,16,64,1024]{3,2,0,1:T(8,128)(2,1)}), bf16[2,16,64,1024]{3,2,0,1:T(8,128)(2,1)}, u32[]{:S(2)}, u32[]{:S(2)}) async-start(bf16[2,16,64,1024]{3,2,0,1:T(8,128)(2,1)} %copy.55), calls=%async_computation.1 | async-start | bytes 8388608 | tf_op jit(solution)/shard_map/all_to_all | solution.py:146
  312.7 56.0 %all-to-all-done.1 = bf16[2,16,64,1024]{3,2,0,1:T(8,128)(2,1)} async-done(((bf16[2,16,64,1024]{3,2,0,1:T(8,128)(2,1)}), bf16[2,16,64,1024]{3,2,0,1:T(8,128)(2,1)}, u32[]{:S(2)}, u32[]{:S(2)}) %all-to-all-start.1) | async-done | bytes 4194336 | tf_op jit(solution)/shard_map/all_to_all | solution.py:146
  368.8 8.9 %gather_fusion.1 = bf16[1024,1024]{1,0:T(8,128)(2,1)} fusion(bf16[2048,1024]{1,0:T(8,128)(2,1)} %bitcast.27, s32[1024]{0:T(1024)S(1)} %broadcast_clamp_fusion), kind=kCustom, calls=%fused_computation.1 | custom fusion | bytes 4198400 | tf_op jit(solution)/shard_map/gather | solution.py:154
  377.7 2.3 fusion.10
  (80 shorter events, 19.1 us)
Async XLA Ops:
  6.5 4.3 %copy-start = (bf16[1024,1024]{1,0:T(8,128)(2,1)S(1)}, bf16[1024,1024]{1,0:T(8,128)(2,1)}, u32[]{:S(2)}) copy-start(bf16[1024,1024]{1,0:T(8,128)(2,1)} %param.17) | copy-start | bytes 6291460
  6.5 6.0 %copy-start.9 = (s32[2]{0:T(128)S(1)}, s32[2]{0:T(128)}, u32[]{:S(2)}) copy-start(s32[2]{0:T(128)} %param.21) | copy-start | bytes 28
  6.5 51.5 %all-gather.10.cloned.1.call-start = ((), (), s32[]{:S(2)}) async-start(), calls=%async_computation.3 | async-start | bytes 1114112 | tf_op jit(solution)/shard_map/all_gather | solution.py:72
  8.2 99.2 %all-gather.14.cloned.1.call-start = ((), (), s32[]{:S(2)}) async-start(), calls=%async_computation.5 | async-start | bytes 1114112 | tf_op jit(solution)/shard_map/all_gather | solution.py:76
  9.7 142.1 %all-gather.8.cloned.1.call-start = ((), (), s32[]{:S(2)}) async-start(), calls=%async_computation.2 | async-start | bytes 2359296 | tf_op jit(solution)/shard_map/all_gather | solution.py:87
  10.9 97.1 %copy-start.8 = (s32[2,16]{1,0:T(2,128)S(1)}, s32[2,16]{1,0:T(2,128)}, u32[]{:S(2)}) copy-start(s32[2,16]{1,0:T(2,128)} %param.20) | copy-start | bytes 388
  14.9 156.4 %all-gather.12.cloned.1.call-start = ((), (), s32[]{:S(2)}) async-start(), calls=%async_computation.4 | async-start | bytes 3145728 | tf_op jit(solution)/shard_map/all_gather | solution.py:71
  58.1 141.5 %all-gather.16.cloned.1.call-start = ((), (), s32[]{:S(2)}) async-start(), calls=%async_computation.6 | async-start | bytes 3145728 | tf_op jit(solution)/shard_map/all_gather | solution.py:75
  107.4 177.1 %all-gather.18.cloned.1.call-start = ((), (), s32[]{:S(2)}) async-start(), calls=%async_computation.7 | async-start | bytes 4456448 | tf_op jit(solution)/shard_map/all_gather | solution.py:78
  123.6 1.7 copy-start.4
  158.6 12.7 %copy-start.2 = (bf16[128,1024]{1,0:T(8,128)(2,1)S(1)}, bf16[128,1024]{1,0:T(8,128)(2,1)}, u32[]{:S(2)}) copy-start(bf16[128,1024]{1,0:T(8,128)(2,1)} %param.13) | copy-start | bytes 786436
  158.6 12.7 %copy-start.5 = (f32[1024]{0:T(1024)S(1)}, f32[1024]{0:T(1024)}, u32[]{:S(2)}) copy-start(f32[1024]{0:T(1024)} %param.14) | copy-start | bytes 12292
  162.9 10.9 %copy-start.3 = (pred[128,3072]{0,1:T(8,128)(4,1)S(1)}, pred[128,3072]{0,1:T(8,128)(4,1)}, u32[]{:S(2)}) copy-start(pred[128,3072]{0,1:T(8,128)(4,1)} %compare_select_fusion) | copy-start | bytes 1179652
  187.8 13.9 %copy-start.6 = (f32[1024]{0:T(1024)S(1)}, f32[1024]{0:T(1024)}, u32[]{:S(2)}) copy-start(f32[1024]{0:T(1024)} %param.15) | copy-start | bytes 12292
  210.0 69.7 %all-to-all-start = ((bf16[16,2,64,1024]{3,2,1,0:T(8,128)(2,1)}), bf16[16,2,64,1024]{3,2,1,0:T(8,128)(2,1)}, u32[]{:S(2)}, u32[]{:S(2)}) async-start(bf16[16,2,64,1024]{3,2,1,0:T(8,128)(2,1)} %bitcast.73), calls=%async_computation | async-start | bytes 8388608 | tf_op jit(solution)/shard_map/all_to_all | solution.py:133
  217.2 78.6 %all-gather.20.cloned.1.call-start = ((), (), s32[]{:S(2)}) async-start(), calls=%async_computation.8 | async-start | bytes 2228224 | tf_op jit(solution)/shard_map/all_gather | solution.py:79
  304.7 7.9 %copy-start.7 = (f32[128,8]{0,1:T(8,128)S(1)}, f32[128,8]{0,1:T(8,128)}, u32[]{:S(2)}) copy-start(f32[128,8]{0,1:T(8,128)} %param.23) | copy-start | bytes 12292
  304.7 64.1 %all-to-all-start.1 = ((bf16[2,16,64,1024]{3,2,0,1:T(8,128)(2,1)}), bf16[2,16,64,1024]{3,2,0,1:T(8,128)(2,1)}, u32[]{:S(2)}, u32[]{:S(2)}) async-start(bf16[2,16,64,1024]{3,2,0,1:T(8,128)(2,1)} %copy.55), calls=%async_computation.1 | async-start | bytes 8388608 | tf_op jit(solution)/shard_map/all_to_all | solution.py:146
  368.8 12.0 %copy-start.1 = (bf16[1024,1024]{1,0:T(8,128)(2,1)S(1)}, bf16[1024,1024]{1,0:T(8,128)(2,1)}, u32[]{:S(2)}) copy-start(bf16[1024,1024]{1,0:T(8,128)(2,1)} %param.17) | copy-start | bytes 6291460
Sparse Core Ops, SparseCore 0:
  9.8 48.2 all-gather.9
  60.5 46.8 all-gather.13
  109.2 42.6 all-gather.7
  153.5 17.7 all-gather.11
  172.9 17.1 all-gather.15
  191.9 43.1 all-gather.17
  236.9 38.0 all-gather.19
where the time goes:
time: 388 us
  waiting for transfers between devices  242 us (62%)
  matrix products  51.6 us (13%)
  local copies, waits for them, and re-layouts  49.4 us (13%)
  starting transfers between devices  15.3 us (4%)
  other arithmetic  14.5 us (4%)
  between operations  14.4 us (4%)
    all_to_all x1, waiting for transfers between devices, shards(): lax.all_to_all(send_buffer.reshape(tp_size, experts_local, capacity, D),...  61.8 us
    all_to_all x1, waiting for transfers between devices, shards(): lax.all_to_all(produced.reshape(experts_local, tp_size, capacity, D), TP,...  56 us
    all_gather x1, waiting for transfers between devices, shards(): lax.all_gather(wo_half, TP, axis=0, tiled=True)  49.3 us
    all_gather x1, waiting for transfers between devices, shards(): lax.all_gather(wq_half, TP, axis=1, tiled=True)  43.1 us
    all_gather x1, waiting for transfers between devices, shards(): request_kv = lax.all_gather(new_kv, 'rb', axis=0, tiled=True)  22.4 us
    sub x1, matrix products, shards(): weights = jnp.exp(scores - top_score)  14 us
    gather x2, local copies, waits for them, and re-layouts, shards(): jnp.take(kv_cache, local_pages, axis=0).reshape(MAX_CACHED, 2 * kv_cols)  12.1 us
    dot_general x1, matrix products, shards(): jnp.einsum('gpqk,kgd->qgpd', probs, values_total, preferred_element_type=...  11.7 us
  transfers between devices with their start and end apart: 9, of which 6 were waited for; matrix products, arithmetic and copies ran while one was open for 24% of the time, Pallas kernels for 0%

commit v1 on v0

--- a/solution.py
+++ b/solution.py
@@ -68,8 +68,14 @@
     group_size = HEADS // KV_HEADS
     half_rows = D // 2
     wq_half = lax.dynamic_slice_in_dim(w_query, core * half_rows, half_rows, 0)
-    wq_full = lax.all_gather(
-        lax.all_gather(wq_half, TP, axis=1, tiled=True), "tc", axis=0, tiled=True
+    wq_full = jnp.concatenate(
+        lax.all_to_all(
+            jnp.stack([lax.all_gather(wq_half, TP, axis=1, tiled=True)] * lax.axis_size("tc")),
+            "tc",
+            0,
+            0,
+        ),
+        axis=0,
     )
     wo_half = lax.dynamic_slice_in_dim(w_out, core * half_rows, half_rows, 1)
     wo_full = lax.all_gather(

time: 388 us -> 361 us (0.930)
  waiting for transfers between devices: 242 us -> 202 us
  blocking collectives: 0 us -> 6.45 us
  local copies, waits for them, and re-layouts: 49.4 us -> 54.3 us
    all_gather x1, waiting for transfers between devices: 43.1 us -> 26.7 us  [shards(): lax.all_gather(wq_half, TP, axis=1, tiled=True)]
    all_to_all x1, waiting for transfers between devices: 61.8 us -> 48.2 us  [shards(): lax.all_to_all(send_buffer.reshape(tp_size, experts_local, capacity, D),...]
    all_gather x1, waiting for transfers between devices: 22.4 us -> 31.8 us  [shards(): request_kv = lax.all_gather(new_kv, 'rb', axis=0, tiled=True)]
    all_gather x1 -> x0, waiting for transfers between devices: 8.38 us -> none  [shards(): lax.all_gather(lax.all_gather(wq_half, TP, axis=1, tiled=True), 'tc', axi...]
    all_to_all x0 -> x1, blocking collectives: none -> 6.45 us  [shards(): lax.all_to_all(jnp.stack([lax.all_gather(wq_half, TP, axis=1, tiled=True)...]
    all_gather x1, waiting for transfers between devices: 49.3 us -> 43 us  [shards(): lax.all_gather(wo_half, TP, axis=0, tiled=True)]
    all_to_all x1, waiting for transfers between devices: 56 us -> 51.6 us  [shards(): lax.all_to_all(produced.reshape(experts_local, tp_size, capacity, D), TP,...]
  transfers between devices with their start and end apart: 9 -> 8, of which waited for: 6 -> 5; matrix products, arithmetic and copies ran while one was open for 24% -> 27% of each run, Pallas kernels for 0% -> 0%
where the time goes in v1:
time: 361 us; the launch traced here: 358 us
  waiting for transfers between devices  202 us (56%)
  local copies, waits for them, and re-layouts  54.3 us (15%)
  matrix products  49.8 us (14%)
  other arithmetic  15.4 us (4%)
  starting transfers between devices  15.1 us (4%)
  between operations  14.5 us (4%)
  blocking collectives  6.45 us (2%)
    all_to_all x1, waiting for transfers between devices, shards(): lax.all_to_all(produced.reshape(experts_local, tp_size, capacity, D), TP,...  51.6 us
    all_to_all x1, waiting for transfers between devices, shards(): lax.all_to_all(send_buffer.reshape(tp_size, experts_local, capacity, D),...  48.2 us
    all_gather x1, waiting for transfers between devices, shards(): lax.all_gather(wo_half, TP, axis=0, tiled=True)  43 us
    all_gather x1, waiting for transfers between devices, shards(): request_kv = lax.all_gather(new_kv, 'rb', axis=0, tiled=True)  31.8 us
    all_gather x1, waiting for transfers between devices, shards(): lax.all_gather(wq_half, TP, axis=1, tiled=True)  26.7 us
    sub x1, matrix products, shards(): weights = jnp.exp(scores - top_score)  14 us
    gather x2, local copies, waits for them, and re-layouts, shards(): jnp.take(kv_cache, local_pages, axis=0).reshape(MAX_CACHED, 2 * kv_cols)  12.1 us
    dot_general x1, matrix products, shards(): jnp.einsum('gpqk,kgd->qgpd', probs, values_total, preferred_element_type=...  11.5 us
  transfers between devices with their start and end apart: 8, of which 5 were waited for; matrix products, arithmetic and copies ran while one was open for 27% of the time, Pallas kernels for 0%

profile of v1, /device:TPU:28, one launch (start us, length us, event | category | flops | bytes accessed | tf_op | source)
XLA Modules:
  0.0 357.9 jit_solution(3078815719426229397)
XLA Ops:
  15.1 43.0 %all-gather.11.cloned.1.call-done = bf16[1024,512]{1,0:T(8,128)(2,1)} async-done(((bf16[64,512]{1,0:T(8,128)(2,1)}), bf16[1024,512]{1,0:T(8,128)(2,1)}) %all-gather.11.cloned.1.call-update) | async-done | bytes 1048592 | tf_op jit(solution)/shard_map/all_gather | solution.py:82
  59.5 5.6 %gather_fusion = bf16[16,128,1024]{2,1,0:T(8,128)(2,1)} fusion(bf16[24,128,1024]{2,1,0:T(8,128)(2,1)} %param.19, s32[1024]{0:T(1024)S(1)} %pad_clamp_fusion), kind=kCustom, calls=%fused_computation | custom fusion | bytes 8388672 | tf_op jit(solution)/shard_map/jit(_take)/gather | solution.py:98
  65.0 6.6 %copy.46 = bf16[2048,1024]{0,1:T(8,128)(2,1)} copy(bf16[2048,1024]{1,0:T(8,128)(2,1)} %bitcast.81) | data formatting | bytes 8388608 | tf_op jit(solution)/shard_map/jit(_take)/gather | solution.py:98
  71.6 2.6 broadcast_select_fusion
  74.3 2.3 fusion.34
  77.2 3.6 compare_select_fusion
  80.7 26.7 %all-gather.9.cloned.1.call-done = bf16[512,1024]{0,1:T(8,128)(2,1)} async-done(((bf16[512,64]{0,1:T(8,128)(2,1)}), bf16[512,1024]{0,1:T(8,128)(2,1)}) %all-gather.9.cloned.1.call-update) | async-done | bytes 1048592 | tf_op jit(solution)/shard_map/all_gather | solution.py:73
  109.1 6.5 %all_to_all.35 = bf16[2,512,1024]{2,1,0:T(8,128)(2,1)} all-to-all(bf16[2,512,1024]{2,1,0:T(8,128)(2,1)S(1)} %pad_maximum_fusion.2), channel_id=1, replica_groups=mesh['tz'=8,'tc'=2,'ra'=2,'rb'=8] {'tc'}, dimensions={0} | all-to-all | bytes 4194304 | tf_op jit(solution)/shard_map/all_to_all | solution.py:72
  115.6 2.9 copy.52
  120.1 31.8 %all-gather.7.cloned.1.call-done = bf16[1024,1024]{1,0:T(8,128)(2,1)} async-done(((bf16[128,1024]{1,0:T(8,128)(2,1)}), bf16[1024,1024]{1,0:T(8,128)(2,1)}) %all-gather.7.cloned.1.call-update) | async-done | bytes 2097168 | tf_op jit(solution)/shard_map/all_gather | solution.py:93
  151.9 3.0 fusion.35
  158.6 4.3 %pad_maximum_fusion = (bf16[3072,512]{0,1:T(8,128)(2,1)}, bf16[3072,512]{0,1:T(8,128)(2,1)}) fusion(bf16[1024,512]{0,1:T(8,128)(2,1)S(1)} %copy.49, bf16[2048,512]{0,1:T(8,128)(2,1)} %get-tuple-element.6, bf16[1024,512]{0,1:T(8,128)(2,1)} %copy.50, bf16[2048,512]{0,1:T(8,128)(2,1)S(1)} %copy-done.2), kind=kLoop, calls=%fused_computation.15 | loop fusion | flops 12582912 | bytes 12582912 | tf_op jit(solution)/shard_map/concatenate | solution.py:102
  162.9 14.0 %fusion.36 = (f32[8,2,128]{2,1,0:T(2,128)S(1)}, f32[8,2,128,3072]{2,3,1,0:T(8,128)}) fusion(pred[128,3072]{0,1:T(8,128)(4,1)} %compare_select_fusion, bf16[3072,8,64,1]{0,2,3,1:T(8,128)(2,1)} %bitcast.88, bf16[128,8,2,64]{0,3,2,1:T(8,128)(2,1)} %bitcast.91), kind=kOutput, calls=%fused_computation.82 | convolution fusion | flops 830475264 | bytes 28975104 | tf_op jit(solution)/shard_map/sub | solution.py:119
  176.8 11.5 %fusion.18 = bf16[8,64,2,128]{3,1,2,0:T(8,128)(2,1)S(1)} fusion(bf16[3072,8,64,1]{0,2,3,1:T(8,128)(2,1)} %bitcast.87, f32[8,2,128,3072]{2,3,1,0:T(8,128)} %get-tuple-element.16, f32[8,2,128]{2,1,0:T(2,128)S(1)} %get-tuple-element.15), kind=kOutput, calls=%fused_computation.30 | convolution fusion | flops 818020352 | bytes 28581888 | tf_op jit(solution)/shard_map/gpqk,kgd->qgpd/dot_general | solution.py:122
  190.7 7.9 %scatter_custom_fusion = bf16[2048,1024]{1,0:T(8,128)(2,1)} fusion(s32[1024]{0:T(1024)S(1)} %reshape.208, bf16[]{:T(256)} %constant.75.clone.1, bf16[128,1024]{1,0:T(8,128)(2,1)S(1)} %multiply_convert_fusion), kind=kCustom, calls=%fused_computation.22 | custom fusion | bytes 4456450 | tf_op jit(solution)/shard_map/scatter | solution.py:138
  198.6 7.8 %all-to-all-start.1 = ((bf16[16,2,64,1024]{3,2,1,0:T(8,128)(2,1)}), bf16[16,2,64,1024]{3,2,1,0:T(8,128)(2,1)}, u32[]{:S(2)}, u32[]{:S(2)}) async-start(bf16[16,2,64,1024]{3,2,1,0:T(8,128)(2,1)} %bitcast.80), calls=%async_computation.1 | async-start | bytes 8388608 | tf_op jit(solution)/shard_map/all_to_all | solution.py:139
  207.0 48.2 %all-to-all-done.1 = bf16[16,2,64,1024]{3,2,1,0:T(8,128)(2,1)} async-done(((bf16[16,2,64,1024]{3,2,1,0:T(8,128)(2,1)}), bf16[16,2,64,1024]{3,2,1,0:T(8,128)(2,1)}, u32[]{:S(2)}, u32[]{:S(2)}) %all-to-all-start.1) | async-done | bytes 4194336 | tf_op jit(solution)/shard_map/all_to_all | solution.py:139
  255.2 4.9 %copy.58 = bf16[1,2,16,64,1024]{4,3,2,1,0:T(8,128)(2,1)} copy(bf16[1,2,16,64,1024]{4,3,1,2,0:T(8,128)(2,1)} %bitcast.26) | data formatting | bytes 8388608 | tf_op jit(solution)/shard_map/all_to_all | solution.py:139
  260.1 11.2 %fusion.37 = f32[2,1024,1024]{2,1,0:T(8,128)} fusion(bf16[2,1024,1024]{2,1,0:T(8,128)(2,1)} %bitcast.85, bf16[2,1024,1024]{2,1,0:T(8,128)(2,1)} %all-gather.15.cloned.1.call-done), kind=kOutput, calls=%fused_computation.83 | convolution fusion | flops 4294967296 | bytes 16777216 | tf_op jit(solution)/shard_map/esd,edf->esf/dot_general | solution.py:147
  271.3 6.4 %convolution_convert_fusion = bf16[2,1024,1024]{2,1,0:T(8,128)(2,1)S(1)} fusion(bf16[2,512,1024]{2,1,0:T(8,128)(2,1)} %all-gather.17.cloned.1.call-done, f32[2,1024,1024]{2,1,0:T(8,128)} %fusion.37), kind=kOutput, calls=%fused_computation.18 | convolution fusion | flops 2155872256 | bytes 14680064 | tf_op jit(solution)/shard_map/esf,efd->esd/dot_general | solution.py:149
  277.7 2.5 copy.59
  280.2 7.1 %all-to-all-start.2 = ((bf16[2,16,64,1024]{3,2,0,1:T(8,128)(2,1)}), bf16[2,16,64,1024]{3,2,0,1:T(8,128)(2,1)}, u32[]{:S(2)}, u32[]{:S(2)}) async-start(bf16[2,16,64,1024]{3,2,0,1:T(8,128)(2,1)} %copy.59), calls=%async_computation.2 | async-start | bytes 8388608 | tf_op jit(solution)/shard_map/all_to_all | solution.py:152
  287.4 51.6 %all-to-all-done.2 = bf16[2,16,64,1024]{3,2,0,1:T(8,128)(2,1)} async-done(((bf16[2,16,64,1024]{3,2,0,1:T(8,128)(2,1)}), bf16[2,16,64,1024]{3,2,0,1:T(8,128)(2,1)}, u32[]{:S(2)}, u32[]{:S(2)}) %all-to-all-start.2) | async-done | bytes 4194336 | tf_op jit(solution)/shard_map/all_to_all | solution.py:152
  339.0 8.9 %gather_fusion.1 = bf16[1024,1024]{1,0:T(8,128)(2,1)} fusion(bf16[2048,1024]{1,0:T(8,128)(2,1)} %bitcast.31, s32[1024]{0:T(1024)S(1)} %broadcast_clamp_fusion), kind=kCustom, calls=%fused_computation.1 | custom fusion | bytes 4198400 | tf_op jit(solution)/shard_map/gather | solution.py:160
  (81 shorter events, 22.8 us)
Async XLA Ops:
  6.5 4.4 %copy-start = (bf16[1024,1024]{1,0:T(8,128)(2,1)S(1)}, bf16[1024,1024]{1,0:T(8,128)(2,1)}, u32[]{:S(2)}) copy-start(bf16[1024,1024]{1,0:T(8,128)(2,1)} %param.17) | copy-start | bytes 6291460
  6.5 6.0 %copy-start.9 = (s32[2]{0:T(128)S(1)}, s32[2]{0:T(128)}, u32[]{:S(2)}) copy-start(s32[2]{0:T(128)} %param.21) | copy-start | bytes 28
  6.5 52.1 %copy-start.8 = (s32[2,16]{1,0:T(2,128)S(1)}, s32[2,16]{1,0:T(2,128)}, u32[]{:S(2)}) copy-start(s32[2,16]{1,0:T(2,128)} %param.20) | copy-start | bytes 388
  6.5 51.5 %all-gather.11.cloned.1.call-start = ((), (), s32[]{:S(2)}) async-start(), calls=%async_computation.5 | async-start | bytes 1114112 | tf_op jit(solution)/shard_map/all_gather | solution.py:82
  8.2 99.2 %all-gather.9.cloned.1.call-start = ((), (), s32[]{:S(2)}) async-start(), calls=%async_computation.4 | async-start | bytes 1114112 | tf_op jit(solution)/shard_map/all_gather | solution.py:73
  9.7 142.1 %all-gather.7.cloned.1.call-start = ((), (), s32[]{:S(2)}) async-start(), calls=%async_computation.3 | async-start | bytes 2359296 | tf_op jit(solution)/shard_map/all_gather | solution.py:93
  15.0 173.4 %all-gather.13.cloned.1.call-start = ((), (), s32[]{:S(2)}) async-start(), calls=%async_computation.6 | async-start | bytes 3145728 | tf_op jit(solution)/shard_map/all_gather | solution.py:81
  58.1 202.0 %all-gather.15.cloned.1.call-start = ((), (), s32[]{:S(2)}) async-start(), calls=%async_computation.7 | async-start | bytes 4456448 | tf_op jit(solution)/shard_map/all_gather | solution.py:84
  74.3 2.3 copy-start.4
  109.1 9.3 %copy-start.3 = (bf16[128,1024]{1,0:T(8,128)(2,1)S(1)}, bf16[128,1024]{1,0:T(8,128)(2,1)}, u32[]{:S(2)}) copy-start(bf16[128,1024]{1,0:T(8,128)(2,1)} %param.13) | copy-start | bytes 786436
  109.1 9.3 %copy-start.5 = (f32[1024]{0:T(1024)S(1)}, f32[1024]{0:T(1024)}, u32[]{:S(2)}) copy-start(f32[1024]{0:T(1024)} %param.14) | copy-start | bytes 12292
  120.1 38.6 %copy-start.2 = (bf16[2048,512]{0,1:T(8,128)(2,1)S(1)}, bf16[2048,512]{0,1:T(8,128)(2,1)}, u32[]{:S(2)}) copy-start(bf16[2048,512]{0,1:T(8,128)(2,1)} %get-tuple-element.5) | copy-start | bytes 6291460
  176.8 13.7 %copy-start.6 = (f32[1024]{0:T(1024)S(1)}, f32[1024]{0:T(1024)}, u32[]{:S(2)}) copy-start(f32[1024]{0:T(1024)} %param.15) | copy-start | bytes 12292
  198.6 56.6 %all-to-all-start.1 = ((bf16[16,2,64,1024]{3,2,1,0:T(8,128)(2,1)}), bf16[16,2,64,1024]{3,2,1,0:T(8,128)(2,1)}, u32[]{:S(2)}, u32[]{:S(2)}) async-start(bf16[16,2,64,1024]{3,2,1,0:T(8,128)(2,1)} %bitcast.80), calls=%async_computation.1 | async-start | bytes 8388608 | tf_op jit(solution)/shard_map/all_to_all | solution.py:139
  206.4 64.9 %all-gather.17.cloned.1.call-start = ((), (), s32[]{:S(2)}) async-start(), calls=%async_computation.8 | async-start | bytes 2228224 | tf_op jit(solution)/shard_map/all_gather | solution.py:85
  280.2 7.1 %copy-start.7 = (f32[128,8]{0,1:T(8,128)S(1)}, f32[128,8]{0,1:T(8,128)}, u32[]{:S(2)}) copy-start(f32[128,8]{0,1:T(8,128)} %param.23) | copy-start | bytes 12292
  280.2 58.8 %all-to-all-start.2 = ((bf16[2,16,64,1024]{3,2,0,1:T(8,128)(2,1)}), bf16[2,16,64,1024]{3,2,0,1:T(8,128)(2,1)}, u32[]{:S(2)}, u32[]{:S(2)}) async-start(bf16[2,16,64,1024]{3,2,0,1:T(8,128)(2,1)} %copy.59), calls=%async_computation.2 | async-start | bytes 8388608 | tf_op jit(solution)/shard_map/all_to_all | solution.py:152
  339.0 12.0 %copy-start.1 = (bf16[1024,1024]{1,0:T(8,128)(2,1)S(1)}, bf16[1024,1024]{1,0:T(8,128)(2,1)}, u32[]{:S(2)}) copy-start(bf16[1024,1024]{1,0:T(8,128)(2,1)} %param.17) | copy-start | bytes 6291460
Sparse Core Ops, SparseCore 0:
  9.8 48.2 all-gather.10
  60.5 46.8 all-gather.8
  109.2 42.6 all-gather.6
  153.5 17.7 all-gather.12
  173.0 43.1 all-gather.14
  217.9 38.0 all-gather.16
